TPU v7x, 128 devices: a whole 4x4x4 slice. The times are simulated.
128 devices in a mesh: tok: 8 (over z, core), wid: 16 (over y, x).
Axes of the slice: x: 4, y: 4, z: 4, core: 2. Of those that a mesh axis runs over, the one named last changes fastest.
Arguments:
- tokens: bfloat16 [8192, 3072], P('tok', 'wid'), may hold values from -6 to 6
- defect_mask: int32 [8192], P('tok'), may hold values 0 or 1
- timestep: int32 [1], replicated, may hold values from 0 to 999
- mask_embed: bfloat16 [3072], P('wid'), may hold values from -6 to 6
- mod_weight: bfloat16 [256, 3, 3072], P(None, None, 'wid'), may hold values from -0.375 to 0.375
- w_qkv: bfloat16 [3072, 3, 2048], P('tok', None, 'wid'), may hold values from -1.4614179 to 1.4614179, as said below
- w_out: bfloat16 [2048, 3072], P('wid'), may hold values from -0.125 to 0.125
Outputs:
- block_out: bfloat16 [8192, 3072], P('tok', 'wid')
Inputs may be any that keep to these rules, and one draw needn't show every extreme that they name: `w_qkv`: entries are at most 81 / sqrt(3072) in magnitude.
All inputs are finite; a program needn't handle non-finite values. No bound on the sum of `defect_mask` on one device may be relied on, other than what follows from the above.
Results may differ from a plain program's by a relative error of at most 0.011.
Values may be sent and summed in bfloat16 or wider, within the bound.
No kernel may reach another device: no remote copies, remote signals or barrier semaphores. Data moves between devices by JAX's collectives and lax.ppermute only.
A program may use at most 128 MiB of HBM per device.

v0:
```python
import math
import jax
import jax.numpy as jnp
from jax import lax
from jax.sharding import PartitionSpec as P

D = 3072
DH = 128
TEMB = 256


def finish_rows(values, row_mean, row_var, shift_row, scale_row):
    normal = (values - row_mean) * lax.rsqrt(row_var + 1e-06)
    return (normal * (1.0 + scale_row.astype(jnp.float32)) + shift_row.astype(jnp.float32)).astype(
        jnp.bfloat16
    )


def body(tokens, defect_mask, timestep, mask_embed, mod_weight, w_qkv, w_out):
    tok_rows = tokens.shape[0]
    residual_in = (
        tokens.astype(jnp.float32)
        + defect_mask.astype(jnp.float32)[:, None] * mask_embed.astype(jnp.float32)[None, :]
    ).astype(jnp.bfloat16)
    w_cols = lax.all_to_all(w_out, "wid", split_axis=1, concat_axis=0, tiled=True)
    tok_count = lax.axis_size("tok")
    w_copies = jnp.broadcast_to(w_qkv[None], (tok_count,) + w_qkv.shape)
    w_full = lax.all_to_all(w_copies, "tok", split_axis=0, concat_axis=0, tiled=True)
    w_full = w_full.reshape((tok_count * w_qkv.shape[0],) + w_qkv.shape[1:])
    half_width = TEMB // 2
    frequency = jnp.exp(-math.log(10000.0) * jnp.arange(half_width, dtype=jnp.float32) / half_width)
    angles = timestep.astype(jnp.float32)[0] * frequency
    embedding = jnp.concatenate([jnp.cos(angles), jnp.sin(angles)])
    modulation = jnp.einsum(
        "e,ecf->cf",
        jax.nn.silu(embedding),
        mod_weight.astype(jnp.float32),
        precision=lax.Precision.HIGHEST,
    ).astype(jnp.bfloat16)
    extra = jnp.zeros((16, residual_in.shape[1]), jnp.bfloat16).at[:2].set(modulation[:2])
    packed = lax.all_gather(
        jnp.concatenate([residual_in, extra], axis=0), "wid", axis=1, tiled=True
    )
    residual_full = packed[:tok_rows]
    shift_scale = packed[tok_rows : tok_rows + 2]
    values = residual_full.astype(jnp.float32)
    row_mean = jnp.mean(values, axis=1, keepdims=True)
    row_var = jnp.mean(values * values, axis=1, keepdims=True) - row_mean * row_mean
    normed = finish_rows(
        values, row_mean, row_var, shift_scale[0][None, :], shift_scale[1][None, :]
    )
    qkv = jnp.einsum("td,dcf->tcf", normed, w_full, preferred_element_type=jnp.float32).astype(
        jnp.bfloat16
    )
    qkv, w_cols = lax.optimization_barrier((qkv, w_cols))
    queries = qkv[:, 0]
    key_values = lax.all_gather(qkv[:, 1:3], "tok", axis=0, tiled=True)
    key_part = key_values[:, 0]
    value_part = key_values[:, 1]
    score_scale = DH ** (-0.5)
    scores = jnp.dot(queries, key_part.T, preferred_element_type=jnp.float32) * score_scale
    shifted = jnp.exp(scores - jnp.max(scores, axis=1, keepdims=True))
    row_sum = jnp.sum(shifted, axis=1, keepdims=True)
    numer = jnp.dot(shifted.astype(jnp.bfloat16), value_part, preferred_element_type=jnp.float32)
    attended = (numer / row_sum).astype(jnp.bfloat16)
    attended_full = lax.all_gather(attended, "wid", axis=1, tiled=True)
    projected = jnp.dot(attended_full, w_cols, preferred_element_type=jnp.float32)
    return (
        residual_in.astype(jnp.float32) + modulation[2].astype(jnp.float32)[None, :] * projected
    ).astype(jnp.bfloat16)


def solution(mesh):
    return jax.shard_map(
        body,
        mesh=mesh,
        in_specs=(
            P("tok", "wid"),
            P("tok"),
            P(),
            P("wid"),
            P(None, None, "wid"),
            P("tok", None, "wid"),
            P("wid", None),
        ),
        out_specs=P("tok", "wid"),
        check_vma=False,
    )
```

profile of v0, /device:TPU:0, one launch (start us, length us, event | category | flops | bytes accessed | tf_op | source)
XLA Modules:
  0.0 239.3 jit_solution(12590052405980159787)
XLA Ops:
  7.3 0.7 convert_element_type.48
  8.0 0.7 convert_element_type.47
  8.7 0.3 fusion.32
  9.0 0.2 copy.16
  9.2 1.2 add_convert_fusion
  10.4 0.0 copy-start.2
  10.4 0.7 copy-done.2
  11.1 0.8 fusion.26
  11.9 0.0 all-gather.4.cloned.1.call-update
  11.9 1.5 copy.14
  13.4 25.8 %all_to_all.24 = bf16[128,16,192]{0,2,1:T(8,128)(2,1)S(1)} all-to-all(bf16[128,16,192]{0,2,1:T(8,128)(2,1)S(1)} %bitcast.41), channel_id=1, replica_groups=mesh['tok'=8,'wid'=16] {'wid'}, dimensions={1} | all-to-all | bytes 1572864 | tf_op jit(solution)/shard_map/all_to_all | solution.py:25
  39.3 2.9 %broadcast_in_dim.2 = bf16[8,384,3,128]{3,1,2,0:T(8,128)(2,1)} broadcast(bf16[384,3,128]{2,0,1:T(8,128)(2,1)} %param.14), dimensions={1,2,3} | broadcast | bytes 2654208 | tf_op jit(solution)/shard_map/broadcast_in_dim | solution.py:27
  42.2 5.8 %all-to-all-start = ((bf16[8,384,3,128]{3,1,2,0:T(8,128)(2,1)}), bf16[8,384,3,128]{3,1,2,0:T(8,128)(2,1)S(1)}, u32[]{:S(2)}, u32[]{:S(2)}) async-start(bf16[8,384,3,128]{3,1,2,0:T(8,128)(2,1)} %broadcast_in_dim.2), calls=%async_computation | async-start | bytes 4718592 | tf_op jit(solution)/shard_map/all_to_all | solution.py:28
  48.0 0.0 all-gather.6.cloned.1.call-start
  48.1 1.0 copy_bitcast_fusion
  49.1 28.9 %all-to-all-done = bf16[8,384,3,128]{3,1,2,0:T(8,128)(2,1)S(1)} async-done(((bf16[8,384,3,128]{3,1,2,0:T(8,128)(2,1)}), bf16[8,384,3,128]{3,1,2,0:T(8,128)(2,1)S(1)}, u32[]{:S(2)}, u32[]{:S(2)}) %all-to-all-start) | async-done | bytes 2359328 | tf_op jit(solution)/shard_map/all_to_all | solution.py:28
  78.0 1.6 copy.12
  79.6 3.2 %all-gather.4.cloned.1.call-done = bf16[1040,3072]{0,1:T(8,128)(2,1)} async-done(((bf16[1040,192]{0,1:T(8,128)(2,1)}), bf16[1040,3072]{0,1:T(8,128)(2,1)}) %all-gather.4.cloned.1.call-update) | async-done | bytes 6389776 | tf_op jit(solution)/shard_map/all_gather | solution.py:41
  82.9 4.6 %convert_reduce_fusion = (f32[1024]{0:T(1024)S(1)}, f32[1024]{0:T(1024)S(1)}) fusion(bf16[1040,3072]{0,1:T(8,128)(2,1)} %all-gather.4.cloned.1.call-done), kind=kLoop, calls=%fused_computation.6 | loop fusion | flops 12580864 | bytes 6299648 | tf_op jit(solution)/shard_map/reduce_sum | solution.py:47
  87.5 2.5 %add_reduce_fusion = (f32[3072]{0:T(1024)S(1)}, f32[3072]{0:T(1024)S(1)}) fusion(bf16[1040,3072]{0,1:T(8,128)(2,1)} %all-gather.4.cloned.1.call-done), kind=kLoop, calls=%fused_computation.20 | loop fusion | flops 9216 | bytes 36864 | tf_op jit(solution)/shard_map/add | solution.py:14
  90.0 5.6 %fusion.14 = bf16[1024,3,128]{2,0,1:T(8,128)(2,1)S(1)} fusion(bf16[3072,3,128]{2,0,1:T(8,128)(2,1)} %bitcast.42, f32[3072]{0:T(1024)S(1)} %get-tuple-element.24, f32[3072]{0:T(1024)S(1)} %get-tuple-element.23, f32[1024]{0:T(1024)S(1)} %get-tuple-element.26, f32[1024]{0:T(1024)S(1)} %get-tuple-element.25, bf16[1040,3072]{0,1:T(8,128)(2,1)S(1)} %copy-done.1), kind=kOutput, calls=%fused_computation.21 | convolution fusion | flops 2435186688 | bytes 9469952 | tf_op jit(solution)/shard_map/td,dcf->tcf/dot_general | solution.py:52
  95.6 0.8 slice.52
  96.4 0.0 all-gather.6.cloned.1.call-update
  96.4 0.2 all-gather.8.cloned.1.call-start
  96.7 31.9 %all-gather.6.cloned.1.call-done = bf16[8192,2,128]{2,0,1:T(8,128)(2,1)} async-done(((bf16[1024,2,128]{2,0,1:T(8,128)(2,1)}), bf16[8192,2,128]{2,0,1:T(8,128)(2,1)}) %all-gather.6.cloned.1.call-update) | async-done | bytes 4194320 | tf_op jit(solution)/shard_map/all_gather | solution.py:57
  128.6 14.6 %multiply_reduce_fusion = (f32[1024]{0:T(1024)S(1)}, f32[1024,8192]{1,0:T(8,128)}) fusion(bf16[8192,2,128]{2,0,1:T(8,128)(2,1)} %all-gather.6.cloned.1.call-done, bf16[1024,3,128]{2,0,1:T(8,128)(2,1)S(1)} %fusion.14), kind=kOutput, calls=%fused_computation.1 | convolution fusion | flops 2164259840 | bytes 35917824 | tf_op jit(solution)/shard_map/dot_general | solution.py:61
  143.2 14.3 %fusion = f32[1024]{0:T(1024)S(1)} fusion(f32[1024,8192]{1,0:T(8,128)} %get-tuple-element.28, f32[1024]{0:T(1024)S(1)} %get-tuple-element.27), kind=kLoop, calls=%fused_computation.2 | loop fusion | flops 25164800 | bytes 33562624 | tf_op jit(solution)/shard_map/reduce_sum | solution.py:63
  157.5 14.2 %fusion.22 = bf16[1024,128]{1,0:T(8,128)(2,1)} fusion(bf16[8192,2,128]{2,0,1:T(8,128)(2,1)S(1)} %copy-done.4, f32[1024,8192]{1,0:T(8,128)} %get-tuple-element.28, f32[1024]{0:T(1024)S(1)} %get-tuple-element.27, f32[1024]{0:T(1024)S(1)} %fusion), kind=kOutput, calls=%fused_computation.26 | convolution fusion | flops 2172911616 | bytes 35921920 | tf_op jit(solution)/shard_map/dot_general | solution.py:64
  171.7 0.0 all-gather.8.cloned.1.call-update
  171.7 0.2 convert_reduce_fusion.2
  171.9 56.4 %all-gather.8.cloned.1.call-done = bf16[1024,2048]{1,0:T(8,128)(2,1)} async-done(((bf16[1024,128]{1,0:T(8,128)(2,1)}), bf16[1024,2048]{1,0:T(8,128)(2,1)}) %all-gather.8.cloned.1.call-update) | async-done | bytes 4194320 | tf_op jit(solution)/shard_map/all_gather | solution.py:66
  228.3 4.5 %fusion.18 = bf16[1024,192]{0,1:T(8,128)(2,1)} fusion(bf16[1024,2048]{1,0:T(8,128)(2,1)} %all-gather.8.cloned.1.call-done, bf16[2048,192]{0,1:T(8,128)(2,1)S(1)} %copy-done.5, bf16[1024,192]{0,1:T(8,128)(2,1)S(1)} %copy-done.3, f32[192]{0:T(256)S(1)} %convert_reduce_fusion.2), kind=kOutput, calls=%fused_computation.24 | convolution fusion | flops 806092800 | bytes 5767936 | tf_op jit(solution)/shard_map/dot_general | solution.py:67
  (14 shorter events, 0.1 us)
Async XLA Ops:
  6.5 2.1 copy-start
  6.5 76.3 %all-gather.4.cloned.1.call-start = ((), (), s32[]{:S(2)}) async-start(), calls=%async_computation.2 | async-start | bytes 7520256 | tf_op jit(solution)/shard_map/all_gather | solution.py:41
  10.4 0.7 copy-start.2
  42.2 35.8 %all-to-all-start = ((bf16[8,384,3,128]{3,1,2,0:T(8,128)(2,1)}), bf16[8,384,3,128]{3,1,2,0:T(8,128)(2,1)S(1)}, u32[]{:S(2)}, u32[]{:S(2)}) async-start(bf16[8,384,3,128]{3,1,2,0:T(8,128)(2,1)} %broadcast_in_dim.2), calls=%async_computation | async-start | bytes 4718592 | tf_op jit(solution)/shard_map/all_to_all | solution.py:28
  48.0 80.5 %all-gather.6.cloned.1.call-start = ((), (), s32[]{:S(2)}) async-start(), calls=%async_computation.3 | async-start | bytes 4718592 | tf_op jit(solution)/shard_map/all_gather | solution.py:57
  82.9 7.1 %copy-start.1 = (bf16[1040,3072]{0,1:T(8,128)(2,1)S(1)}, bf16[1040,3072]{0,1:T(8,128)(2,1)}, u32[]{:S(2)}) copy-start(bf16[1040,3072]{0,1:T(8,128)(2,1)} %all-gather.4.cloned.1.call-done) | copy-start | bytes 19169284
  96.4 131.9 %all-gather.8.cloned.1.call-start = ((), (), s32[]{:S(2)}) async-start(), calls=%async_computation.4 | async-start | bytes 4456448 | tf_op jit(solution)/shard_map/all_gather | solution.py:66
  143.2 14.3 %copy-start.4 = (bf16[8192,2,128]{2,0,1:T(8,128)(2,1)S(1)}, bf16[8192,2,128]{2,0,1:T(8,128)(2,1)}, u32[]{:S(2)}) copy-start(bf16[8192,2,128]{2,0,1:T(8,128)(2,1)} %all-gather.6.cloned.1.call-done) | copy-start | bytes 12582916
  157.5 70.9 %copy-start.3 = (bf16[1024,192]{0,1:T(8,128)(2,1)S(1)}, bf16[1024,192]{0,1:T(8,128)(2,1)}, u32[]{:S(2)}) copy-start(bf16[1024,192]{0,1:T(8,128)(2,1)} %copy-done.2) | copy-start | bytes 1179652
  157.5 70.8 %copy-start.5 = (bf16[2048,192]{0,1:T(8,128)(2,1)S(1)}, bf16[2048,192]{0,1:T(8,128)(2,1)}, u32[]{:S(2)}) copy-start(bf16[2048,192]{0,1:T(8,128)(2,1)} %copy_bitcast_fusion) | copy-start | bytes 2359300
Sparse Core Ops, SparseCore 0:
  12.1 70.7 all-gather.3
  96.6 31.9 all-gather.5
  171.8 56.4 all-gather.7
where the time goes:
time: 240 us; the launch traced here: 239 us
  waiting for transfers between devices  121 us (50%)
  matrix products  39.2 us (16%)
  blocking collectives  25.8 us (11%)
  other arithmetic  24.9 us (10%)
  between operations  13.9 us (6%)
  local copies, waits for them, and re-layouts  8.83 us (4%)
  starting transfers between devices  6.07 us (3%)
    all_gather x1, waiting for transfers between devices, body(): attended_full = lax.all_gather(attended, 'wid', axis=1, tiled=True)  56.4 us
    all_gather x1, waiting for transfers between devices, body(): key_values = lax.all_gather(qkv[:, 1:3], 'tok', axis=0, tiled=True)  31.9 us
    all_to_all x1, waiting for transfers between devices, body(): lax.all_to_all(w_copies, 'tok', split_axis=0, concat_axis=0, tiled=True)  28.9 us
    all_to_all x1, blocking collectives, body(): lax.all_to_all(w_out, 'wid', split_axis=1, concat_axis=0, tiled=True)  25.8 us
    dot_general x1, matrix products, body(): jnp.dot(queries, key_part.T, preferred_element_type=jnp.float32)  14.6 us
    reduce_sum x1, other arithmetic, body(): row_sum = jnp.sum(shifted, axis=1, keepdims=True)  14.3 us
    dot_general x1, matrix products, body(): jnp.dot(shifted.astype(jnp.bfloat16), value_part, preferred_element_type=...  14.2 us
    all_to_all x1, starting transfers between devices, body(): lax.all_to_all(w_copies, 'tok', split_axis=0, concat_axis=0, tiled=True)  5.81 us
  transfers between devices with their start and end apart: 4, of which 4 were waited for; matrix products, arithmetic and copies ran while one was open for 3% of the time, Pallas kernels for 0%

commit v1 on v0

--- a/solution.py
+++ b/solution.py
@@ -7,6 +7,28 @@
 D = 3072
 DH = 128
 TEMB = 256
+
+
+def draft_sheet(unit):
+    base_arr = jax.lax.psum(1, "wid")
+    main, k_now, later = (base_arr, jax.lax.axis_index("wid"), unit.shape[1])
+    entries = []
+    for tick in range(main):
+        entries.append((tick, (tick + 1) % main))
+    arrivals = []
+    for tick in range(main):
+        arrivals.append((tick, (tick - 1) % main))
+    aux = jnp.zeros((*unit.shape[:1], main * later, *unit.shape[2:]), unit.dtype)
+    aux = lax.dynamic_update_slice_in_dim(aux, unit, k_now * later, axis=1)
+    back = carry = unit
+    f_now = main // 2
+    for nth in range(1, f_now + 1):
+        back = jax.lax.ppermute(back, "wid", entries)
+        aux = lax.dynamic_update_slice_in_dim(aux, back, (k_now - nth) % main * later, axis=1)
+        if nth < main - f_now:
+            carry = jax.lax.ppermute(carry, "wid", arrivals)
+            aux = lax.dynamic_update_slice_in_dim(aux, carry, (k_now + nth) % main * later, axis=1)
+    return aux
 
 
 def finish_rows(values, row_mean, row_var, shift_row, scale_row):
@@ -63,7 +85,7 @@
     row_sum = jnp.sum(shifted, axis=1, keepdims=True)
     numer = jnp.dot(shifted.astype(jnp.bfloat16), value_part, preferred_element_type=jnp.float32)
     attended = (numer / row_sum).astype(jnp.bfloat16)
-    attended_full = lax.all_gather(attended, "wid", axis=1, tiled=True)
+    attended_full = draft_sheet(attended)
     projected = jnp.dot(attended_full, w_cols, preferred_element_type=jnp.float32)
     return (
         residual_in.astype(jnp.float32) + modulation[2].astype(jnp.float32)[None, :] * projected

time: 240 us -> 270 us (1.12)
  starting transfers between devices: 6.07 us -> 43.5 us
  waiting for transfers between devices: 121 us -> 98.9 us
  local copies, waits for them, and re-layouts: 8.83 us -> 22.8 us
    all_gather x1 -> x0, waiting for transfers between devices: 56.4 us -> none  [body(): attended_full = lax.all_gather(attended, 'wid', axis=1, tiled=True)]
    ppermute x0 -> x15, starting transfers between devices: none -> 37.6 us  [the longest x7 36.2 us: draft_sheet(): carry = jax.lax.ppermute(carry, 'wid', arrivals)]
    ppermute x0 -> x15, waiting for transfers between devices: none -> 33.6 us  [the longest x8 33.6 us: draft_sheet(): back = jax.lax.ppermute(back, 'wid', entries)]
    dynamic_update_slice x0 -> x15, local copies, waits for them, and re-layouts: none -> 11.3 us  [the longest x8 5.96 us: draft_sheet(): lax.dynamic_update_slice_in_dim(aux, back, (k_now - nth) % main * later,...]
  transfers between devices with their start and end apart: 4 -> 18, of which waited for: 4 -> 11; matrix products, arithmetic and copies ran while one was open for 3% -> 6% of each run, Pallas kernels for 0% -> 0%
where the time goes in v1:
time: 270 us; the launch traced here: 269 us
  waiting for transfers between devices  98.9 us (37%)
  starting transfers between devices  43.5 us (16%)
  matrix products  39.2 us (15%)
  blocking collectives  25.8 us (10%)
  other arithmetic  24.6 us (9%)
  local copies, waits for them, and re-layouts  22.8 us (8%)
  between operations  14.5 us (5%)
    ppermute x7, starting transfers between devices, draft_sheet(): carry = jax.lax.ppermute(carry, 'wid', arrivals)  36.2 us
    ppermute x8, waiting for transfers between devices, draft_sheet(): back = jax.lax.ppermute(back, 'wid', entries)  33.6 us
    all_gather x1, waiting for transfers between devices, body(): key_values = lax.all_gather(qkv[:, 1:3], 'tok', axis=0, tiled=True)  32.1 us
    all_to_all x1, waiting for transfers between devices, body(): lax.all_to_all(w_copies, 'tok', split_axis=0, concat_axis=0, tiled=True)  28.9 us
    all_to_all x1, blocking collectives, body(): lax.all_to_all(w_out, 'wid', split_axis=1, concat_axis=0, tiled=True)  25.8 us
    dot_general x1, matrix products, body(): jnp.dot(queries, key_part.T, preferred_element_type=jnp.float32)  14.7 us
    dot_general x1, matrix products, body(): jnp.dot(shifted.astype(jnp.bfloat16), value_part, preferred_element_type=...  14.1 us
    reduce_sum x1, other arithmetic, body(): row_sum = jnp.sum(shifted, axis=1, keepdims=True)  14.1 us
  transfers between devices with their start and end apart: 18, of which 11 were waited for; matrix products, arithmetic and copies ran while one was open for 6% of the time, Pallas kernels for 0%

profile of v1, /device:TPU:0, one launch (start us, length us, event | category | flops | bytes accessed | tf_op | source)
XLA Modules:
  0.0 269.3 jit_solution(11899938288094163206)
XLA Ops:
  12.0 1.5 copy.14
  13.5 25.8 %all_to_all.24 = bf16[128,16,192]{0,2,1:T(8,128)(2,1)S(1)} all-to-all(bf16[128,16,192]{0,2,1:T(8,128)(2,1)S(1)} %bitcast.43), channel_id=1, replica_groups=mesh['tok'=8,'wid'=16] {'wid'}, dimensions={1} | all-to-all | bytes 1572864 | tf_op jit(solution)/shard_map/all_to_all | solution.py:47
  39.3 2.0 broadcast_in_dim.5
  41.3 5.8 %all-to-all-start = ((bf16[8,384,3,128]{3,1,2,0:T(8,128)(2,1)}), bf16[8,384,3,128]{3,1,2,0:T(8,128)(2,1)S(1)}, u32[]{:S(2)}, u32[]{:S(2)}) async-start(bf16[8,384,3,128]{3,1,2,0:T(8,128)(2,1)} %broadcast_in_dim.5), calls=%async_computation | async-start | bytes 4718592 | tf_op jit(solution)/shard_map/all_to_all | solution.py:50
  48.1 28.9 %all-to-all-done = bf16[8,384,3,128]{3,1,2,0:T(8,128)(2,1)S(1)} async-done(((bf16[8,384,3,128]{3,1,2,0:T(8,128)(2,1)}), bf16[8,384,3,128]{3,1,2,0:T(8,128)(2,1)S(1)}, u32[]{:S(2)}, u32[]{:S(2)}) %all-to-all-start) | async-done | bytes 2359328 | tf_op jit(solution)/shard_map/all_to_all | solution.py:50
  77.1 1.6 copy.12
  78.7 4.2 %all-gather.3.cloned.1.call-done = bf16[1040,3072]{0,1:T(8,128)(2,1)} async-done(((bf16[1040,192]{0,1:T(8,128)(2,1)}), bf16[1040,3072]{0,1:T(8,128)(2,1)}) %all-gather.3.cloned.1.call-update) | async-done | bytes 6389776 | tf_op jit(solution)/shard_map/all_gather | solution.py:63
  82.9 4.6 %convert_reduce_fusion = (f32[1024]{0:T(1024)S(1)}, f32[1024]{0:T(1024)S(1)}) fusion(bf16[1040,3072]{0,1:T(8,128)(2,1)} %all-gather.3.cloned.1.call-done), kind=kLoop, calls=%fused_computation.6 | loop fusion | flops 12580864 | bytes 6299648 | tf_op jit(solution)/shard_map/reduce_sum | solution.py:69
  87.5 2.3 add_reduce_fusion
  89.9 5.6 %fusion.14 = bf16[1024,3,128]{2,0,1:T(8,128)(2,1)S(1)} fusion(bf16[3072,3,128]{2,0,1:T(8,128)(2,1)} %bitcast.44, f32[3072]{0:T(1024)S(1)} %get-tuple-element.24, f32[3072]{0:T(1024)S(1)} %get-tuple-element.23, f32[1024]{0:T(1024)S(1)} %get-tuple-element.26, f32[1024]{0:T(1024)S(1)} %get-tuple-element.25, bf16[1040,3072]{0,1:T(8,128)(2,1)S(1)} %copy-done.2), kind=kOutput, calls=%fused_computation.21 | convolution fusion | flops 2435186688 | bytes 9469952 | tf_op jit(solution)/shard_map/td,dcf->tcf/dot_general | solution.py:74
  96.4 32.1 %all-gather.5.cloned.1.call-done = bf16[8192,2,128]{2,0,1:T(8,128)(2,1)} async-done(((bf16[1024,2,128]{2,0,1:T(8,128)(2,1)}), bf16[8192,2,128]{2,0,1:T(8,128)(2,1)}) %all-gather.5.cloned.1.call-update) | async-done | bytes 4194320 | tf_op jit(solution)/shard_map/all_gather | solution.py:79
  128.5 14.7 %multiply_reduce_fusion = (f32[1024]{0:T(1024)S(1)}, f32[1024,8192]{1,0:T(8,128)}) fusion(bf16[8192,2,128]{2,0,1:T(8,128)(2,1)} %all-gather.5.cloned.1.call-done, bf16[1024,3,128]{2,0,1:T(8,128)(2,1)S(1)} %fusion.14), kind=kOutput, calls=%fused_computation.1 | convolution fusion | flops 2164259840 | bytes 35917824 | tf_op jit(solution)/shard_map/dot_general | solution.py:83
  143.2 14.1 %fusion = f32[1024]{0:T(1024)S(1)} fusion(f32[1024,8192]{1,0:T(8,128)} %get-tuple-element.28, f32[1024]{0:T(1024)S(1)} %get-tuple-element.27), kind=kLoop, calls=%fused_computation.2 | loop fusion | flops 25164800 | bytes 33562624 | tf_op jit(solution)/shard_map/reduce_sum | solution.py:85
  157.2 2.7 broadcast_in_dim.4
  160.9 14.1 %constant_dynamic-update-slice_fusion.15 = (bf16[1024,2048]{1,0:T(8,128)(2,1)}, bf16[1024,128]{1,0:T(8,128)(2,1)S(1)}) fusion(bf16[1024,2048]{1,0:T(8,128)(2,1)} %broadcast_in_dim.4, s32[]{:T(128)S(6)} %select_n.111, f32[1024]{0:T(1024)S(1)} %fusion, bf16[8192,2,128]{2,0,1:T(8,128)(2,1)S(1)} %copy-done.5, f32[1024,8192]{1,0:T(8,128)} %get-tuple-element.28, ...), kind=kOutput, calls=%fused_computation.51 | convolution fusion | flops 2172911616 | bytes 36184068 | tf_op jit(solution)/shard_map/dot_general | solution.py:86
  175.0 1.4 collective-permute-start
  176.5 3.9 %collective-permute-start.1 = (bf16[1024,128]{1,0:T(8,128)(2,1)S(1)}, bf16[1024,128]{1,0:T(8,128)(2,1)S(1)}, u32[]{:S(2)}, u32[]{:S(2)}) collective-permute-start(bf16[1024,128]{1,0:T(8,128)(2,1)S(1)} %get-tuple-element.30), channel_id=1, source_target_pairs={{0,15},{1,0},{2,1},{3,2},{4,3},{5,4},{6,5},{7,6},{8,7},{9,8},{10,9... | collective-permute-start | bytes 786440 | tf_op jit(solution)/shard_map/ppermute | solution.py:29
  180.4 6.4 %collective-permute-done = bf16[1024,128]{1,0:T(8,128)(2,1)S(1)} collective-permute-done((bf16[1024,128]{1,0:T(8,128)(2,1)S(1)}, bf16[1024,128]{1,0:T(8,128)(2,1)S(1)}, u32[]{:S(2)}, u32[]{:S(2)}) %collective-permute-start) | collective-permute-done | bytes 262176 | tf_op jit(solution)/shard_map/ppermute | solution.py:26
  186.8 5.3 %collective-permute-start.3 = (bf16[1024,128]{1,0:T(8,128)(2,1)S(1)}, bf16[1024,128]{1,0:T(8,128)(2,1)S(1)}, u32[]{:S(2)}, u32[]{:S(2)}) collective-permute-start(bf16[1024,128]{1,0:T(8,128)(2,1)S(1)} %collective-permute-done.1), channel_id=1, source_target_pairs={{0,15},{1,0},{2,1},{3,2},{4,3},{5,4},{6,5},{7,6},{8,7},{9,8},{10,9... | collective-permute-start | bytes 786440 | tf_op jit(solution)/shard_map/ppermute | solution.py:29
  192.2 5.6 %collective-permute-done.2 = bf16[1024,128]{1,0:T(8,128)(2,1)S(1)} collective-permute-done((bf16[1024,128]{1,0:T(8,128)(2,1)S(1)}, bf16[1024,128]{1,0:T(8,128)(2,1)S(1)}, u32[]{:S(2)}, u32[]{:S(2)}) %collective-permute-start.2) | collective-permute-done | bytes 262176 | tf_op jit(solution)/shard_map/ppermute | solution.py:26
  197.7 5.3 %collective-permute-start.5 = (bf16[1024,128]{1,0:T(8,128)(2,1)S(1)}, bf16[1024,128]{1,0:T(8,128)(2,1)S(1)}, u32[]{:S(2)}, u32[]{:S(2)}) collective-permute-start(bf16[1024,128]{1,0:T(8,128)(2,1)S(1)} %collective-permute-done.3), channel_id=1, source_target_pairs={{0,15},{1,0},{2,1},{3,2},{4,3},{5,4},{6,5},{7,6},{8,7},{9,8},{10,9... | collective-permute-start | bytes 786440 | tf_op jit(solution)/shard_map/ppermute | solution.py:29
  203.1 4.7 %collective-permute-done.4 = bf16[1024,128]{1,0:T(8,128)(2,1)S(1)} collective-permute-done((bf16[1024,128]{1,0:T(8,128)(2,1)S(1)}, bf16[1024,128]{1,0:T(8,128)(2,1)S(1)}, u32[]{:S(2)}, u32[]{:S(2)}) %collective-permute-start.4) | collective-permute-done | bytes 262176 | tf_op jit(solution)/shard_map/ppermute | solution.py:26
  209.0 5.4 %collective-permute-start.7 = (bf16[1024,128]{1,0:T(8,128)(2,1)S(1)}, bf16[1024,128]{1,0:T(8,128)(2,1)S(1)}, u32[]{:S(2)}, u32[]{:S(2)}) collective-permute-start(bf16[1024,128]{1,0:T(8,128)(2,1)S(1)} %collective-permute-done.5), channel_id=1, source_target_pairs={{0,15},{1,0},{2,1},{3,2},{4,3},{5,4},{6,5},{7,6},{8,7},{9,8},{10,9... | collective-permute-start | bytes 786440 | tf_op jit(solution)/shard_map/ppermute | solution.py:29
  215.1 2.4 collective-permute-done.6
  219.0 5.4 %collective-permute-start.9 = (bf16[1024,128]{1,0:T(8,128)(2,1)S(1)}, bf16[1024,128]{1,0:T(8,128)(2,1)S(1)}, u32[]{:S(2)}, u32[]{:S(2)}) collective-permute-start(bf16[1024,128]{1,0:T(8,128)(2,1)S(1)} %collective-permute-done.7), channel_id=1, source_target_pairs={{0,15},{1,0},{2,1},{3,2},{4,3},{5,4},{6,5},{7,6},{8,7},{9,8},{10,9... | collective-permute-start | bytes 786440 | tf_op jit(solution)/shard_map/ppermute | solution.py:29
  225.1 2.1 collective-permute-done.8
  228.7 5.3 %collective-permute-start.11 = (bf16[1024,128]{1,0:T(8,128)(2,1)S(1)}, bf16[1024,128]{1,0:T(8,128)(2,1)S(1)}, u32[]{:S(2)}, u32[]{:S(2)}) collective-permute-start(bf16[1024,128]{1,0:T(8,128)(2,1)S(1)} %collective-permute-done.9), channel_id=1, source_target_pairs={{0,15},{1,0},{2,1},{3,2},{4,3},{5,4},{6,5},{7,6},{8,7},{9,8},{10,9... | collective-permute-start | bytes 786440 | tf_op jit(solution)/shard_map/ppermute | solution.py:29
  234.8 2.1 collective-permute-done.10
  238.4 5.5 %collective-permute-start.13 = (bf16[1024,128]{1,0:T(8,128)(2,1)S(1)}, bf16[1024,128]{1,0:T(8,128)(2,1)S(1)}, u32[]{:S(2)}, u32[]{:S(2)}) collective-permute-start(bf16[1024,128]{1,0:T(8,128)(2,1)S(1)} %collective-permute-done.11), channel_id=1, source_target_pairs={{0,15},{1,0},{2,1},{3,2},{4,3},{5,4},{6,5},{7,6},{8,7},{9,8},{10,9... | collective-permute-start | bytes 786440 | tf_op jit(solution)/shard_map/ppermute | solution.py:29
  244.6 2.9 %collective-permute-done.12 = bf16[1024,128]{1,0:T(8,128)(2,1)S(1)} collective-permute-done((bf16[1024,128]{1,0:T(8,128)(2,1)S(1)}, bf16[1024,128]{1,0:T(8,128)(2,1)S(1)}, u32[]{:S(2)}, u32[]{:S(2)}) %collective-permute-start.12) | collective-permute-done | bytes 262176 | tf_op jit(solution)/shard_map/ppermute | solution.py:26
  249.9 7.4 %collective-permute-done.14 = bf16[1024,128]{1,0:T(8,128)(2,1)S(1)} collective-permute-done((bf16[1024,128]{1,0:T(8,128)(2,1)S(1)}, bf16[1024,128]{1,0:T(8,128)(2,1)S(1)}, u32[]{:S(2)}, u32[]{:S(2)}) %collective-permute-start.14) | collective-permute-done | bytes 262176 | tf_op jit(solution)/shard_map/ppermute | solution.py:26
  258.0 4.5 %fusion.18 = bf16[1024,192]{0,1:T(8,128)(2,1)} fusion(bf16[1024,2048]{1,0:T(8,128)(2,1)} %constant_dynamic-update-slice_fusion, bf16[2048,192]{0,1:T(8,128)(2,1)S(1)} %copy-done.6, bf16[1024,192]{0,1:T(8,128)(2,1)S(1)} %copy-done.4, f32[192]{0:T(256)S(1)} %convert_reduce_fusion.2), kind=kOutput, calls=%fused_computation.24 | convolution fusion | flops 806092800 | bytes 5767936 | tf_op jit(solution)/shard_map/dot_general | solution.py:89
  (61 shorter events, 19.1 us)
Async XLA Ops:
  6.5 2.1 copy-start
  6.5 32.8 %copy-start.7 = (bf16[384,3,128]{2,0,1:T(8,128)(2,1)S(1)}, bf16[384,3,128]{2,0,1:T(8,128)(2,1)}, u32[]{:S(2)}) copy-start(bf16[384,3,128]{2,0,1:T(8,128)(2,1)} %param.14) | copy-start | bytes 884740
  6.5 76.4 %all-gather.3.cloned.1.call-start = ((), (), s32[]{:S(2)}) async-start(), calls=%async_computation.2 | async-start | bytes 7520256 | tf_op jit(solution)/shard_map/all_gather | solution.py:63
  10.4 0.7 copy-start.3
  41.3 35.8 %all-to-all-start = ((bf16[8,384,3,128]{3,1,2,0:T(8,128)(2,1)}), bf16[8,384,3,128]{3,1,2,0:T(8,128)(2,1)S(1)}, u32[]{:S(2)}, u32[]{:S(2)}) async-start(bf16[8,384,3,128]{3,1,2,0:T(8,128)(2,1)} %broadcast_in_dim.5), calls=%async_computation | async-start | bytes 4718592 | tf_op jit(solution)/shard_map/all_to_all | solution.py:50
  47.1 81.4 %all-gather.5.cloned.1.call-start = ((), (), s32[]{:S(2)}) async-start(), calls=%async_computation.3 | async-start | bytes 4718592 | tf_op jit(solution)/shard_map/all_gather | solution.py:79
  82.9 7.0 %copy-start.2 = (bf16[1040,3072]{0,1:T(8,128)(2,1)S(1)}, bf16[1040,3072]{0,1:T(8,128)(2,1)}, u32[]{:S(2)}) copy-start(bf16[1040,3072]{0,1:T(8,128)(2,1)} %all-gather.3.cloned.1.call-done) | copy-start | bytes 19169284
  157.2 3.7 %copy-start.5 = (bf16[8192,2,128]{2,0,1:T(8,128)(2,1)S(1)}, bf16[8192,2,128]{2,0,1:T(8,128)(2,1)}, u32[]{:S(2)}) copy-start(bf16[8192,2,128]{2,0,1:T(8,128)(2,1)} %all-gather.5.cloned.1.call-done) | copy-start | bytes 12582916
  175.0 83.0 %copy-start.4 = (bf16[1024,192]{0,1:T(8,128)(2,1)S(1)}, bf16[1024,192]{0,1:T(8,128)(2,1)}, u32[]{:S(2)}) copy-start(bf16[1024,192]{0,1:T(8,128)(2,1)} %copy-done.3) | copy-start | bytes 1179652
  175.0 83.0 %copy-start.6 = (bf16[2048,192]{0,1:T(8,128)(2,1)S(1)}, bf16[2048,192]{0,1:T(8,128)(2,1)}, u32[]{:S(2)}) copy-start(bf16[2048,192]{0,1:T(8,128)(2,1)} %copy_bitcast_fusion) | copy-start | bytes 2359300
  175.0 11.8 %collective-permute-start = (bf16[1024,128]{1,0:T(8,128)(2,1)S(1)}, bf16[1024,128]{1,0:T(8,128)(2,1)S(1)}, u32[]{:S(2)}, u32[]{:S(2)}) collective-permute-start(bf16[1024,128]{1,0:T(8,128)(2,1)S(1)} %get-tuple-element.30), channel_id=1, source_target_pairs={{0,1},{1,2},{2,3},{3,4},{4,5},{5,6},{6,7},{7,8},{8,9},{9,10},{10,1... | collective-permute-start | bytes 786440 | tf_op jit(solution)/shard_map/ppermute | solution.py:26
  176.5 10.3 %collective-permute-start.1 = (bf16[1024,128]{1,0:T(8,128)(2,1)S(1)}, bf16[1024,128]{1,0:T(8,128)(2,1)S(1)}, u32[]{:S(2)}, u32[]{:S(2)}) collective-permute-start(bf16[1024,128]{1,0:T(8,128)(2,1)S(1)} %get-tuple-element.30), channel_id=1, source_target_pairs={{0,15},{1,0},{2,1},{3,2},{4,3},{5,4},{6,5},{7,6},{8,7},{9,8},{10,9... | collective-permute-start | bytes 786440 | tf_op jit(solution)/shard_map/ppermute | solution.py:29
  186.8 10.9 %collective-permute-start.2 = (bf16[1024,128]{1,0:T(8,128)(2,1)S(1)}, bf16[1024,128]{1,0:T(8,128)(2,1)S(1)}, u32[]{:S(2)}, u32[]{:S(2)}) collective-permute-start(bf16[1024,128]{1,0:T(8,128)(2,1)S(1)} %collective-permute-done), channel_id=1, source_target_pairs={{0,1},{1,2},{2,3},{3,4},{4,5},{5,6},{6,7},{7,8},{8,9},{9,10},{10,1... | collective-permute-start | bytes 786440 | tf_op jit(solution)/shard_map/ppermute | solution.py:26
  186.8 10.9 %collective-permute-start.3 = (bf16[1024,128]{1,0:T(8,128)(2,1)S(1)}, bf16[1024,128]{1,0:T(8,128)(2,1)S(1)}, u32[]{:S(2)}, u32[]{:S(2)}) collective-permute-start(bf16[1024,128]{1,0:T(8,128)(2,1)S(1)} %collective-permute-done.1), channel_id=1, source_target_pairs={{0,15},{1,0},{2,1},{3,2},{4,3},{5,4},{6,5},{7,6},{8,7},{9,8},{10,9... | collective-permute-start | bytes 786440 | tf_op jit(solution)/shard_map/ppermute | solution.py:29
  197.7 10.1 %collective-permute-start.4 = (bf16[1024,128]{1,0:T(8,128)(2,1)S(1)}, bf16[1024,128]{1,0:T(8,128)(2,1)S(1)}, u32[]{:S(2)}, u32[]{:S(2)}) collective-permute-start(bf16[1024,128]{1,0:T(8,128)(2,1)S(1)} %collective-permute-done.2), channel_id=1, source_target_pairs={{0,1},{1,2},{2,3},{3,4},{4,5},{5,6},{6,7},{7,8},{8,9},{9,10},{10,1... | collective-permute-start | bytes 786440 | tf_op jit(solution)/shard_map/ppermute | solution.py:26
  197.7 11.2 %collective-permute-start.5 = (bf16[1024,128]{1,0:T(8,128)(2,1)S(1)}, bf16[1024,128]{1,0:T(8,128)(2,1)S(1)}, u32[]{:S(2)}, u32[]{:S(2)}) collective-permute-start(bf16[1024,128]{1,0:T(8,128)(2,1)S(1)} %collective-permute-done.3), channel_id=1, source_target_pairs={{0,15},{1,0},{2,1},{3,2},{4,3},{5,4},{6,5},{7,6},{8,7},{9,8},{10,9... | collective-permute-start | bytes 786440 | tf_op jit(solution)/shard_map/ppermute | solution.py:29
  207.8 9.7 %collective-permute-start.6 = (bf16[1024,128]{1,0:T(8,128)(2,1)S(1)}, bf16[1024,128]{1,0:T(8,128)(2,1)S(1)}, u32[]{:S(2)}, u32[]{:S(2)}) collective-permute-start(bf16[1024,128]{1,0:T(8,128)(2,1)S(1)} %collective-permute-done.4), channel_id=1, source_target_pairs={{0,1},{1,2},{2,3},{3,4},{4,5},{5,6},{6,7},{7,8},{8,9},{9,10},{10,1... | collective-permute-start | bytes 786440 | tf_op jit(solution)/shard_map/ppermute | solution.py:26
  209.0 10.0 %collective-permute-start.7 = (bf16[1024,128]{1,0:T(8,128)(2,1)S(1)}, bf16[1024,128]{1,0:T(8,128)(2,1)S(1)}, u32[]{:S(2)}, u32[]{:S(2)}) collective-permute-start(bf16[1024,128]{1,0:T(8,128)(2,1)S(1)} %collective-permute-done.5), channel_id=1, source_target_pairs={{0,15},{1,0},{2,1},{3,2},{4,3},{5,4},{6,5},{7,6},{8,7},{9,8},{10,9... | collective-permute-start | bytes 786440 | tf_op jit(solution)/shard_map/ppermute | solution.py:29
  217.5 9.7 %collective-permute-start.8 = (bf16[1024,128]{1,0:T(8,128)(2,1)S(1)}, bf16[1024,128]{1,0:T(8,128)(2,1)S(1)}, u32[]{:S(2)}, u32[]{:S(2)}) collective-permute-start(bf16[1024,128]{1,0:T(8,128)(2,1)S(1)} %collective-permute-done.6), channel_id=1, source_target_pairs={{0,1},{1,2},{2,3},{3,4},{4,5},{5,6},{6,7},{7,8},{8,9},{9,10},{10,1... | collective-permute-start | bytes 786440 | tf_op jit(solution)/shard_map/ppermute | solution.py:26
  219.0 9.7 %collective-permute-start.9 = (bf16[1024,128]{1,0:T(8,128)(2,1)S(1)}, bf16[1024,128]{1,0:T(8,128)(2,1)S(1)}, u32[]{:S(2)}, u32[]{:S(2)}) collective-permute-start(bf16[1024,128]{1,0:T(8,128)(2,1)S(1)} %collective-permute-done.7), channel_id=1, source_target_pairs={{0,15},{1,0},{2,1},{3,2},{4,3},{5,4},{6,5},{7,6},{8,7},{9,8},{10,9... | collective-permute-start | bytes 786440 | tf_op jit(solution)/shard_map/ppermute | solution.py:29
  227.2 9.7 %collective-permute-start.10 = (bf16[1024,128]{1,0:T(8,128)(2,1)S(1)}, bf16[1024,128]{1,0:T(8,128)(2,1)S(1)}, u32[]{:S(2)}, u32[]{:S(2)}) collective-permute-start(bf16[1024,128]{1,0:T(8,128)(2,1)S(1)} %collective-permute-done.8), channel_id=1, source_target_pairs={{0,1},{1,2},{2,3},{3,4},{4,5},{5,6},{6,7},{7,8},{8,9},{9,10},{10,1... | collective-permute-start | bytes 786440 | tf_op jit(solution)/shard_map/ppermute | solution.py:26
  228.7 9.7 %collective-permute-start.11 = (bf16[1024,128]{1,0:T(8,128)(2,1)S(1)}, bf16[1024,128]{1,0:T(8,128)(2,1)S(1)}, u32[]{:S(2)}, u32[]{:S(2)}) collective-permute-start(bf16[1024,128]{1,0:T(8,128)(2,1)S(1)} %collective-permute-done.9), channel_id=1, source_target_pairs={{0,15},{1,0},{2,1},{3,2},{4,3},{5,4},{6,5},{7,6},{8,7},{9,8},{10,9... | collective-permute-start | bytes 786440 | tf_op jit(solution)/shard_map/ppermute | solution.py:29
  236.9 10.7 %collective-permute-start.12 = (bf16[1024,128]{1,0:T(8,128)(2,1)S(1)}, bf16[1024,128]{1,0:T(8,128)(2,1)S(1)}, u32[]{:S(2)}, u32[]{:S(2)}) collective-permute-start(bf16[1024,128]{1,0:T(8,128)(2,1)S(1)} %collective-permute-done.10), channel_id=1, source_target_pairs={{0,1},{1,2},{2,3},{3,4},{4,5},{5,6},{6,7},{7,8},{8,9},{9,10},{10,1... | collective-permute-start | bytes 786440 | tf_op jit(solution)/shard_map/ppermute | solution.py:26
  238.4 10.7 %collective-permute-start.13 = (bf16[1024,128]{1,0:T(8,128)(2,1)S(1)}, bf16[1024,128]{1,0:T(8,128)(2,1)S(1)}, u32[]{:S(2)}, u32[]{:S(2)}) collective-permute-start(bf16[1024,128]{1,0:T(8,128)(2,1)S(1)} %collective-permute-done.11), channel_id=1, source_target_pairs={{0,15},{1,0},{2,1},{3,2},{4,3},{5,4},{6,5},{7,6},{8,7},{9,8},{10,9... | collective-permute-start | bytes 786440 | tf_op jit(solution)/shard_map/ppermute | solution.py:29
  247.6 9.7 %collective-permute-start.14 = (bf16[1024,128]{1,0:T(8,128)(2,1)S(1)}, bf16[1024,128]{1,0:T(8,128)(2,1)S(1)}, u32[]{:S(2)}, u32[]{:S(2)}) collective-permute-start(bf16[1024,128]{1,0:T(8,128)(2,1)S(1)} %collective-permute-done.12), channel_id=1, source_target_pairs={{0,1},{1,2},{2,3},{3,4},{4,5},{5,6},{6,7},{7,8},{8,9},{9,10},{10,1... | collective-permute-start | bytes 786440 | tf_op jit(solution)/shard_map/ppermute | solution.py:26
  247.6 14.9 %copy-start.1 = (bf16[256,3,192]{0,2,1:T(8,128)(2,1)S(1)}, bf16[256,3,192]{0,2,1:T(8,128)(2,1)}, u32[]{:S(2)}) copy-start(bf16[256,3,192]{0,2,1:T(8,128)(2,1)} %param.13) | copy-start | bytes 884740
Sparse Core Ops, SparseCore 0:
  12.1 70.7 all-gather.2
  96.5 31.9 all-gather.4
